TPU v7x, 32 devices: a whole 2x2x4 slice. The times are simulated.
32 devices in a mesh: req: 8 (over z, y), tp: 4 (over x, core).
Axes of the slice: x: 2, y: 2, z: 4, core: 2. Of those that a mesh axis runs over, the one named last changes fastest.
Arguments:
- hidden: bfloat16 [4096, 2048], P('req', 'tp'), may hold values from -6 to 6
- queries: bfloat16 [4096, 2048], P('req', 'tp'), may hold values from -4 to 4
- new_keys: bfloat16 [4096, 512], P('req'), may hold values from -4 to 4
- new_values: bfloat16 [4096, 512], P('req'), may hold values from -6 to 6
- cache_keys: bfloat16 [384, 64, 512], P('req'), may hold values from -6 to 6
- cache_values: bfloat16 [384, 64, 512], P('req'), may hold values from -6 to 6
- out_weight: bfloat16 [2048, 2048], P('tp'), may hold values from -0.125 to 0.125
- attn_gain: bfloat16 [2048], P('tp'), may hold values from 0.099609375 to 1.8984375
- ple_input: bfloat16 [4096, 256], P('req'), may hold values from -6 to 6
- ple_gate_weight: bfloat16 [2048, 256], P('tp'), may hold values from -0.125 to 0.125
- ple_proj_weight: bfloat16 [256, 2048], P(None, 'tp'), may hold values from -0.375 to 0.375
- ple_gain: bfloat16 [2048], P('tp'), may hold values from 0.099609375 to 1.8984375
- page_holder: int32 [384, 1], P('req'), may hold values from 0 to 7; in each aligned block of 48 rows (0 to 47, 48 to 95, ...) at most 6 rows name the same one
- page_slot: int32 [384, 1], P('req'), may hold values from 0 to 47
- page_counts: int32 [8, 8], P('req'), may hold values from 1 to 12, 48 in all within a row
- last_fill: int32 [8, 8], P('req'), may hold values from 1 to 64
- row_counts: int32 [8, 8], P('req'), may hold values from 1 to 256, 512 in all within a row
Outputs:
- layer_out: bfloat16 [4096, 2048], P('req', 'tp')
Inputs may be any that keep to these rules, and one draw needn't show every extreme that they name: `page_holder`: within the 48 page references of one device's requests (aligned blocks), no req index is named more than 6 times; in some block one is named exactly 6 times. `page_counts`: the 8 counts of one device sum to 48; some count equals 12. `row_counts`: the 8 counts of one device sum to 512; some count equals 256.
All inputs are finite; a program needn't handle non-finite values.
Results may differ from a plain program's by a relative error of at most 0.0061.
Values may be sent and summed in bfloat16 or wider, within the bound.
No kernel may reach another device: no remote copies, remote signals or barrier semaphores. Data moves between devices by JAX's collectives and lax.ppermute only.
A program may use at most 128 MiB of HBM per device.

v0:
```python
import math
import jax
import jax.numpy as jnp
from jax import lax
from jax.sharding import PartitionSpec as P

D = 2048
HD = 256


def slot_lookup(positions, counts):
    starts = jnp.cumsum(counts) - counts
    owning = jnp.sum((positions[:, None] >= starts[None, :]).astype(jnp.int32), axis=1) - 1
    return (owning, starts)


def table_pick(table, owning):
    onehot = owning[:, None] == jnp.arange(table.shape[0], dtype=jnp.int32)[None, :]
    return jnp.sum(jnp.where(onehot, table[None, :], 0), axis=1)


def attend_masks(counts_of_pages, fill_row, counts_of_rows, page_len, page_total, row_total):
    key_index = jnp.arange(page_total * page_len, dtype=jnp.int32)
    page_ref = key_index // page_len
    within = key_index % page_len
    page_owner, page_starts = slot_lookup(page_ref, counts_of_pages)
    context_len = (counts_of_pages - 1) * page_len + fill_row
    position = (page_ref - table_pick(page_starts, page_owner)) * page_len + within
    valid = position < table_pick(context_len, page_owner)
    row_index = jnp.arange(row_total, dtype=jnp.int32)
    row_owner = slot_lookup(row_index, counts_of_rows)[0]
    context_mask = (row_owner[:, None] == page_owner[None, :]) & valid[None, :]
    causal = (row_owner[:, None] == row_owner[None, :]) & (row_index[None, :] <= row_index[:, None])
    return jnp.concatenate([context_mask, causal], axis=1)


def shards(
    hidden,
    queries,
    new_keys,
    new_values,
    cache_keys,
    cache_values,
    out_weight,
    attn_gain,
    ple_input,
    ple_gate_weight,
    ple_proj_weight,
    ple_gain,
    page_holder,
    page_slot,
    page_counts,
    last_fill,
    row_counts,
):
    row_total = hidden.shape[0]
    page_total = cache_keys.shape[0]
    page_len = cache_keys.shape[1]
    req_count = lax.axis_size("req")
    tp_index = lax.axis_index("tp")
    local_heads = queries.shape[1] // HD
    kv_head = tp_index // 2
    capacity = max(2, page_total // req_count)
    holders = page_holder[:, 0]
    places = page_slot[:, 0]
    ref_index = jnp.arange(page_total, dtype=jnp.int32)
    earlier = (holders[:, None] == holders[None, :]) & (ref_index[:, None] > ref_index[None, :])
    ranking = jnp.sum(earlier.astype(jnp.int32), axis=1)
    matched = (holders[:, None, None] == jnp.arange(req_count, dtype=jnp.int32)[None, :, None]) & (
        ranking[:, None, None] == jnp.arange(capacity, dtype=jnp.int32)[None, None, :]
    )
    request_table = jnp.sum(jnp.where(matched, places[:, None, None] + 1, 0), axis=0) - 1
    asked = lax.all_to_all(request_table, "req", split_axis=0, concat_axis=0, tiled=True)
    wanted = jnp.maximum(asked, 0)
    head_keys = lax.dynamic_slice_in_dim(cache_keys, kv_head * HD, HD, 2)
    head_values = lax.dynamic_slice_in_dim(cache_values, kv_head * HD, HD, 2)
    stacked = jnp.concatenate([head_keys, head_values], axis=2)
    arrival_index = holders * capacity + ranking
    outgoing = stacked[wanted]
    arrived = lax.all_to_all(outgoing, "req", split_axis=0, concat_axis=0, tiled=True)
    context = arrived.reshape(req_count * capacity, page_len, 2 * HD)[arrival_index]
    context_keys = context[:, :, :HD].reshape(page_total * page_len, HD)
    context_values = context[:, :, HD:].reshape(page_total * page_len, HD)
    fresh_keys = lax.dynamic_slice_in_dim(new_keys, kv_head * HD, HD, 1)
    fresh_values = lax.dynamic_slice_in_dim(new_values, kv_head * HD, HD, 1)
    all_keys = jnp.concatenate([context_keys, fresh_keys], axis=0)
    all_values = jnp.concatenate([context_values, fresh_values], axis=0)
    masking = attend_masks(
        page_counts[0], last_fill[0], row_counts[0], page_len, page_total, row_total
    )
    query_rows = queries.reshape(row_total, local_heads, HD)
    scores = jnp.einsum("rhd,kd->hrk", query_rows, all_keys, preferred_element_type=jnp.float32) * (
        1.0 / math.sqrt(HD)
    )
    scores = jnp.where(masking[None], scores, -1e30)
    highest = jnp.max(scores, axis=-1, keepdims=True)
    expo = jnp.exp(scores - highest)
    weights = (expo / jnp.sum(expo, axis=-1, keepdims=True)).astype(jnp.bfloat16)
    attention = jnp.einsum("hrk,kd->rhd", weights, all_values, preferred_element_type=jnp.float32)
    attention = attention.astype(jnp.bfloat16).reshape(row_total, local_heads * HD)
    partial_sum = jnp.dot(attention, out_weight, preferred_element_type=jnp.float32)
    columns = hidden.shape[1]
    summed = lax.psum(partial_sum, "tp")
    squares = jnp.sum(summed * summed, axis=1)
    local_part = lax.dynamic_slice_in_dim(summed, tp_index * columns, columns, 1)
    normed = (
        local_part
        * lax.rsqrt(squares / D + 1e-06)[:, None]
        * attn_gain.astype(jnp.float32)[None, :]
    )
    mixed_state = (hidden.astype(jnp.float32) + normed).astype(jnp.bfloat16)
    gate = lax.psum(jnp.dot(mixed_state, ple_gate_weight, preferred_element_type=jnp.float32), "tp")
    activated = (jax.nn.gelu(gate, approximate=True) * ple_input.astype(jnp.float32)).astype(
        jnp.bfloat16
    )
    lifted = jnp.dot(activated, ple_proj_weight, preferred_element_type=jnp.float32)
    lift_squares = lax.psum(jnp.sum(lifted * lifted, axis=1), "tp")
    lift_normed = (
        lifted
        * lax.rsqrt(lift_squares / D + 1e-06)[:, None]
        * ple_gain.astype(jnp.float32)[None, :]
    )
    return (mixed_state.astype(jnp.float32) + lift_normed).astype(jnp.bfloat16)


def solution(mesh):
    return jax.shard_map(
        shards,
        mesh=mesh,
        in_specs=(
            P("req", "tp"),
            P("req", "tp"),
            P("req", None),
            P("req", None),
            P("req", None, None),
            P("req", None, None),
            P("tp", None),
            P("tp"),
            P("req", None),
            P("tp", None),
            P(None, "tp"),
            P("tp"),
            P("req", None),
            P("req", None),
            P("req", None),
            P("req", None),
            P("req", None),
        ),
        out_specs=P("req", "tp"),
        check_vma=False,
    )
```

profile of v0, /device:TPU:0, one launch (start us, length us, event | category | flops | bytes accessed | tf_op | source)
XLA Modules:
  0.0 293.5 jit_solution(17418125813564555138)
XLA Ops:
  6.5 1.0 convert_reduce_fusion.1
  7.5 0.7 iota_compare_fusion.5
  8.2 0.7 add_bitcast_fusion.2
  9.1 0.7 copy.35
  9.7 7.3 %all-to-all-start = ((s32[8,1,6]{2,1,0:T(1,128)}), s32[8,1,6]{2,1,0:T(1,128)S(1)}, u32[]{:S(2)}, u32[]{:S(2)}) async-start(s32[8,1,6]{2,1,0:T(1,128)} %copy.35), calls=%async_computation | async-start | bytes 8192 | tf_op jit(solution)/shard_map/all_to_all | solution.py:73
  17.0 2.2 constant_dynamic-slice_fusion.2
  19.3 2.0 pad_maximum_fusion
  21.2 2.2 all-to-all-done
  23.5 4.4 %gather_fusion = bf16[48,64,512]{2,1,0:T(8,128)(2,1)} fusion(bf16[48,64,512]{2,1,0:T(8,128)(2,1)} %pad_maximum_fusion, s32[1024]{0:T(1024)S(1)} %pad_clamp_fusion.1), kind=kCustom, calls=%fused_computation | custom fusion | bytes 6291648 | tf_op jit(solution)/shard_map/gather | solution.py:79
  28.0 4.6 %all-to-all-start.1 = ((bf16[8,6,64,512]{3,2,1,0:T(8,128)(2,1)}), bf16[8,6,64,512]{3,2,1,0:T(8,128)(2,1)}, u32[]{:S(2)}, u32[]{:S(2)}) async-start(bf16[8,6,64,512]{3,2,1,0:T(8,128)(2,1)} %bitcast.52), calls=%async_computation.1 | async-start | bytes 6291456 | tf_op jit(solution)/shard_map/all_to_all | solution.py:80
  33.0 1.0 constant_dynamic-slice_fusion
  34.6 0.2 fusion.12
  34.8 2.4 compare_and_fusion
  37.1 1.7 pad_add_fusion
  38.8 63.4 %all-to-all-done.1 = bf16[8,6,64,512]{3,2,1,0:T(8,128)(2,1)} async-done(((bf16[8,6,64,512]{3,2,1,0:T(8,128)(2,1)}), bf16[8,6,64,512]{3,2,1,0:T(8,128)(2,1)}, u32[]{:S(2)}, u32[]{:S(2)}) %all-to-all-start.1) | async-done | bytes 3145760 | tf_op jit(solution)/shard_map/all_to_all | solution.py:80
  102.2 4.4 %gather_fusion.1 = bf16[48,64,512]{2,1,0:T(8,128)(2,1)} fusion(bf16[48,64,512]{2,1,0:T(8,128)(2,1)} %bitcast.4, s32[1024]{0:T(1024)S(1)} %pad_clamp_fusion), kind=kCustom, calls=%fused_computation.1 | custom fusion | bytes 6291648 | tf_op jit(solution)/shard_map/gather | solution.py:81
  106.7 4.0 %fusion.49 = (bf16[48,64,256]{2,1,0:T(8,128)(2,1)}, bf16[48,64,256]{2,1,0:T(8,128)(2,1)}) fusion(bf16[48,64,512]{2,1,0:T(8,128)(2,1)} %gather_fusion.1), kind=kLoop, calls=%fused_computation.97 | loop fusion | bytes 6291456 | tf_op jit(solution)/shard_map/slice | solution.py:83
  110.6 2.7 copy.37
  113.3 8.7 %fusion.8 = f32[3584,512,2]{1,0,2:T(8,128)} fusion(bf16[512,256]{1,0:T(8,128)(2,1)S(1)} %get-tuple-element.15, bf16[3072,256]{1,0:T(8,128)(2,1)} %bitcast.53, bf16[64,2,8,256]{3,2,1,0:T(8,128)(2,1)S(1)} %bitcast.55), kind=kOutput, calls=%fused_computation.19 | convolution fusion | flops 1882718208 | bytes 17039360 | tf_op jit(solution)/shard_map/rhd,kd->hrk/dot_general | solution.py:92
  122.0 17.1 %fusion.50 = (f32[2,512]{1,0:T(2,128)S(1)}, f32[2,512,3584]{1,2,0:T(8,128)}) fusion(f32[3584,512,2]{1,0,2:T(8,128)} %fusion.8, pred[512,3584]{0,1:T(8,128)(4,1)} %pad_add_fusion), kind=kOutput, calls=%fused_computation.98 | output fusion | flops 22023680 | bytes 31199232 | tf_op jit(solution)/shard_map/sub | solution.py:97
  139.1 7.7 %fusion.11 = bf16[256,2,512]{2,0,1:T(8,128)(2,1)S(1)} fusion(f32[2,512,3584]{1,2,0:T(8,128)} %get-tuple-element.12, f32[2,512]{1,0:T(2,128)S(1)} %get-tuple-element.11, bf16[512,256]{0,1:T(8,128)(2,1)S(1)} %copy.44, bf16[3072,256]{0,1:T(8,128)(2,1)} %copy.37), kind=kOutput, calls=%fused_computation.22 | convolution fusion | flops 1890320384 | bytes 17043456 | tf_op jit(solution)/shard_map/hrk,kd->rhd/dot_general | solution.py:99
  146.9 3.2 %fusion.51 = f32[512,2048]{1,0:T(8,128)} fusion(bf16[512,512]{0,1:T(8,128)(2,1)S(1)} %bitcast.56, bf16[512,2048]{1,0:T(8,128)(2,1)S(1)} %copy-done), kind=kOutput, calls=%fused_computation.99 | convolution fusion | flops 1073741824 | bytes 6815744 | tf_op jit(solution)/shard_map/dot_general | solution.py:101
  150.2 0.6 copy-done.5
  150.8 84.0 %all-reduce.3.cloned.1.call-done = f32[512,2048]{1,0:T(8,128)} async-done(((f32[512,2048]{1,0:T(8,128)}), f32[512,2048]{1,0:T(8,128)}) %all-reduce.3.cloned.1.call-update) | async-done | bytes 4194320 | tf_op jit(solution)/shard_map/psum | solution.py:103
  234.8 2.5 multiply_reduce_fusion
  237.4 1.5 add_convert_fusion.1
  238.8 1.1 fusion.52
  240.0 33.5 %all-reduce.5.cloned.1.call-done = f32[512,256]{1,0:T(8,128)} async-done(((f32[512,256]{1,0:T(8,128)}), f32[512,256]{1,0:T(8,128)}) %all-reduce.5.cloned.1.call-update) | async-done | bytes 524304 | tf_op jit(solution)/shard_map/psum | solution.py:112
  273.4 2.7 multiply_reduce_fusion.1
  276.1 2.6 copy.40
  278.7 5.7 %psum.23 = f32[512]{0:T(512)S(1)} all-reduce(f32[512]{0:T(512)S(1)} %get-tuple-element.13), channel_id=1, replica_groups=mesh['req'=8,'tp'=4] {'tp'}, use_global_device_ids=true, to_apply=%region_14.15 | all-reduce | flops 512 | bytes 4096 | tf_op jit(solution)/shard_map/psum | solution.py:117
  284.4 2.2 add_convert_fusion
  (49 shorter events, 1.3 us)
Async XLA Ops:
  6.5 140.3 %copy-start = (bf16[512,2048]{1,0:T(8,128)(2,1)S(1)}, bf16[512,2048]{1,0:T(8,128)(2,1)}, u32[]{:S(2)}) copy-start(bf16[512,2048]{1,0:T(8,128)(2,1)} %param.23) | copy-start | bytes 6291460
  9.7 13.7 %all-to-all-start = ((s32[8,1,6]{2,1,0:T(1,128)}), s32[8,1,6]{2,1,0:T(1,128)S(1)}, u32[]{:S(2)}, u32[]{:S(2)}) async-start(s32[8,1,6]{2,1,0:T(1,128)} %copy.35), calls=%async_computation | async-start | bytes 8192 | tf_op jit(solution)/shard_map/all_to_all | solution.py:73
  28.0 4.7 %copy-start.8 = (s32[1,8]{1,0:T(1,128)S(1)}, s32[1,8]{1,0:T(1,128)}, u32[]{:S(2)}) copy-start(s32[1,8]{1,0:T(1,128)} %param.31) | copy-start | bytes 100
  28.0 4.9 %copy-start.10 = (s32[1,8]{1,0:T(1,128)S(1)}, s32[1,8]{1,0:T(1,128)}, u32[]{:S(2)}) copy-start(s32[1,8]{1,0:T(1,128)} %param.33) | copy-start | bytes 100
  28.0 5.0 %copy-start.4 = (bf16[512,512]{1,0:T(8,128)(2,1)S(1)}, bf16[512,512]{1,0:T(8,128)(2,1)}, u32[]{:S(2)}) copy-start(bf16[512,512]{1,0:T(8,128)(2,1)} %param.19) | copy-start | bytes 1572868
  28.0 6.2 %copy-start.9 = (s32[48,1]{0,1:T(1,128)S(1)}, s32[48,1]{0,1:T(1,128)}, u32[]{:S(2)}) copy-start(s32[48,1]{0,1:T(1,128)} %param.29) | copy-start | bytes 580
  28.0 6.3 %copy-start.7 = (s32[1,8]{1,0:T(1,128)S(1)}, s32[1,8]{1,0:T(1,128)}, u32[]{:S(2)}) copy-start(s32[1,8]{1,0:T(1,128)} %param.32) | copy-start | bytes 100
  28.0 74.2 %all-to-all-start.1 = ((bf16[8,6,64,512]{3,2,1,0:T(8,128)(2,1)}), bf16[8,6,64,512]{3,2,1,0:T(8,128)(2,1)}, u32[]{:S(2)}, u32[]{:S(2)}) async-start(bf16[8,6,64,512]{3,2,1,0:T(8,128)(2,1)} %bitcast.52), calls=%async_computation.1 | async-start | bytes 6291456 | tf_op jit(solution)/shard_map/all_to_all | solution.py:80
  32.6 202.2 %all-reduce.3.cloned.1.call-start = ((), (), s32[]{:S(2)}) async-start(), calls=%async_computation.2 | async-start | bytes 8388608 | tf_op jit(solution)/shard_map/psum | solution.py:103
  110.6 2.7 copy-start.1
  150.1 0.7 copy-start.5
  150.1 87.2 %copy-start.2 = (bf16[512,512]{1,0:T(8,128)(2,1)S(1)}, bf16[512,512]{1,0:T(8,128)(2,1)}, u32[]{:S(2)}) copy-start(bf16[512,512]{1,0:T(8,128)(2,1)} %param.17) | copy-start | bytes 1572868
  150.1 123.3 %all-reduce.5.cloned.1.call-start = ((), (), s32[]{:S(2)}) async-start(), calls=%async_computation.3 | async-start | bytes 1048576 | tf_op jit(solution)/shard_map/psum | solution.py:112
  150.8 88.0 %copy-start.3 = (bf16[512,256]{1,0:T(8,128)(2,1)S(1)}, bf16[512,256]{1,0:T(8,128)(2,1)}, u32[]{:S(2)}) copy-start(bf16[512,256]{1,0:T(8,128)(2,1)} %param.26) | copy-start | bytes 786436
  150.8 89.2 %copy-start.6 = (bf16[512]{0:T(512)(128)(2,1)S(1)}, bf16[512]{0:T(512)(128)(2,1)}, u32[]{:S(2)}) copy-start(bf16[512]{0:T(512)(128)(2,1)} %param.28) | copy-start | bytes 3076
Sparse Core Ops, SparseCore 0:
  150.3 84.5 all-reduce.2
  240.1 33.3 all-reduce.4
where the time goes:
time: 294 us
  waiting for transfers between devices  183 us (62%)
  other arithmetic  32.8 us (11%)
  matrix products  23.5 us (8%)
  local copies, waits for them, and re-layouts  22.9 us (8%)
  between operations  13.6 us (5%)
  starting transfers between devices  11.9 us (4%)
  blocking collectives  5.73 us (2%)
    psum x1, waiting for transfers between devices, shards(): summed = lax.psum(partial_sum, 'tp')  84 us
    all_to_all x1, waiting for transfers between devices, shards(): lax.all_to_all(outgoing, 'req', split_axis=0, concat_axis=0, tiled=True)  63.4 us
    psum x1, waiting for transfers between devices, shards(): lax.psum(jnp.dot(mixed_state, ple_gate_weight, preferred_element_type=jnp...  33.5 us
    sub x1, other arithmetic, shards(): expo = jnp.exp(scores - highest)  17.1 us
    dot_general x1, matrix products, shards(): jnp.einsum('rhd,kd->hrk', query_rows, all_keys, preferred_element_type=jn...  8.73 us
    dot_general x1, matrix products, shards(): jnp.einsum('hrk,kd->rhd', weights, all_values, preferred_element_type=jnp...  7.72 us
    all_to_all x1, starting transfers between devices, shards(): lax.all_to_all(request_table, 'req', split_axis=0, concat_axis=0, tiled=T...  7.28 us
  transfers between devices with their start and end apart: 4, of which 4 were waited for; matrix products, arithmetic and copies ran while one was open for 4% of the time, Pallas kernels for 0%

commit v1 on v0

--- a/solution.py
+++ b/solution.py
@@ -6,6 +6,18 @@
 
 D = 2048
 HD = 256
+
+
+def exchange_directly(shard, axis, split, join):
+    ways, here = (lax.axis_size(axis), lax.axis_index(axis))
+    width = shard.shape[split] // ways
+    turned = jnp.roll(shard, -here * width, axis=split)
+    got = [lax.slice_in_dim(turned, 0, width, axis=split)]
+    for far in range(1, ways):
+        sent = lax.slice_in_dim(turned, far * width, (far + 1) * width, axis=split)
+        got.append(lax.ppermute(sent, axis, [(d, (d + far) % ways) for d in range(ways)]))
+    line = jnp.concatenate(got[::-1], axis=join)
+    return jnp.roll(line, (here + 1) * got[0].shape[join], axis=join)
 
 
 def slot_lookup(positions, counts):
@@ -70,7 +82,7 @@
         ranking[:, None, None] == jnp.arange(capacity, dtype=jnp.int32)[None, None, :]
     )
     request_table = jnp.sum(jnp.where(matched, places[:, None, None] + 1, 0), axis=0) - 1
-    asked = lax.all_to_all(request_table, "req", split_axis=0, concat_axis=0, tiled=True)
+    asked = exchange_directly(request_table, "req", 0, 0)
     wanted = jnp.maximum(asked, 0)
     head_keys = lax.dynamic_slice_in_dim(cache_keys, kv_head * HD, HD, 2)
     head_values = lax.dynamic_slice_in_dim(cache_values, kv_head * HD, HD, 2)

time: 294 us -> 301 us (1.024)
  starting transfers between devices: 11.9 us -> 17.1 us
    ppermute x0 -> x7, starting transfers between devices: none -> 12.4 us  [exchange_directly(): lax.ppermute(sent, axis, [(d, (d + far) % ways) for d in range(ways)])]
    all_to_all x1 -> x0, starting transfers between devices: 7.28 us -> none  [shards(): lax.all_to_all(request_table, 'req', split_axis=0, concat_axis=0, tiled=T...]
    ppermute x0 -> x7, waiting for transfers between devices: none -> 5.17 us  [exchange_directly(): lax.ppermute(sent, axis, [(d, (d + far) % ways) for d in range(ways)])]
  transfers between devices with their start and end apart: 4 -> 10, of which waited for: 4 -> 5; matrix products, arithmetic and copies ran while one was open for 4% -> 3% of each run, Pallas kernels for 0% -> 0%
where the time goes in v1:
time: 301 us; the launch traced here: 300 us
  waiting for transfers between devices  185 us (61%)
  other arithmetic  33 us (11%)
  matrix products  23.5 us (8%)
  local copies, waits for them, and re-layouts  22.5 us (7%)
  starting transfers between devices  17.1 us (6%)
  between operations  13.6 us (5%)
  blocking collectives  5.73 us (2%)
    psum x1, waiting for transfers between devices, shards(): summed = lax.psum(partial_sum, 'tp')  84 us
    all_to_all x1, waiting for transfers between devices, shards(): lax.all_to_all(outgoing, 'req', split_axis=0, concat_axis=0, tiled=True)  61.9 us
    psum x1, waiting for transfers between devices, shards(): lax.psum(jnp.dot(mixed_state, ple_gate_weight, preferred_element_type=jnp...  33.5 us
    sub x1, other arithmetic, shards(): expo = jnp.exp(scores - highest)  17.1 us
    ppermute x7, starting transfers between devices, exchange_directly(): lax.ppermute(sent, axis, [(d, (d + far) % ways) for d in range(ways)])  12.4 us
    dot_general x1, matrix products, shards(): jnp.einsum('rhd,kd->hrk', query_rows, all_keys, preferred_element_type=jn...  8.73 us
    dot_general x1, matrix products, shards(): jnp.einsum('hrk,kd->rhd', weights, all_values, preferred_element_type=jnp...  7.72 us
  transfers between devices with their start and end apart: 10, of which 5 were waited for; matrix products, arithmetic and copies ran while one was open for 3% of the time, Pallas kernels for 0%

profile of v1, /device:TPU:0, one launch (start us, length us, event | category | flops | bytes accessed | tf_op | source)
XLA Modules:
  0.0 300.0 jit_solution(2314647680060880362)
XLA Ops:
  6.5 1.0 convert_reduce_fusion.1
  7.5 0.7 iota_compare_fusion.5
  9.3 6.0 %collective-permute-start = (s32[1,6]{0,1:T(8,128)S(1)}, s32[1,6]{0,1:T(8,128)S(1)}, u32[]{:S(2)}, u32[]{:S(2)}) collective-permute-start(s32[1,6]{0,1:T(8,128)S(1)} %get-tuple-element.17), channel_id=1, source_target_pairs={{0,28},{4,0},{8,4},{12,8},{16,12},{20,16},{24,20},{28,24},{1,29},{... | collective-permute-start | bytes 80 | tf_op jit(solution)/shard_map/ppermute | solution.py:18
  15.8 3.0 collective-permute-start.3
  18.7 2.2 constant_dynamic-slice_fusion.3
  21.0 2.0 pad_maximum_fusion
  23.0 1.9 collective-permute-start.5
  24.8 1.1 collective-permute-start.6
  26.0 3.4 %collective-permute-done.5 = s32[1,6]{0,1:T(8,128)S(1)} collective-permute-done((s32[1,6]{0,1:T(8,128)S(1)}, s32[1,6]{0,1:T(8,128)S(1)}, u32[]{:S(2)}, u32[]{:S(2)}) %collective-permute-start.5) | collective-permute-done | bytes 56 | tf_op jit(solution)/shard_map/ppermute | solution.py:18
  29.3 1.8 collective-permute-done.6
  31.5 4.4 %gather_fusion = bf16[48,64,512]{2,1,0:T(8,128)(2,1)} fusion(bf16[48,64,512]{2,1,0:T(8,128)(2,1)} %pad_maximum_fusion, s32[1024]{0:T(1024)S(1)} %pad_clamp_fusion.1), kind=kCustom, calls=%fused_computation | custom fusion | bytes 6291648 | tf_op jit(solution)/shard_map/gather | solution.py:91
  36.0 4.6 %all-to-all-start = ((bf16[8,6,64,512]{3,2,1,0:T(8,128)(2,1)}), bf16[8,6,64,512]{3,2,1,0:T(8,128)(2,1)}, u32[]{:S(2)}, u32[]{:S(2)}) async-start(bf16[8,6,64,512]{3,2,1,0:T(8,128)(2,1)} %bitcast.50), calls=%async_computation | async-start | bytes 6291456 | tf_op jit(solution)/shard_map/all_to_all | solution.py:92
  41.0 1.0 constant_dynamic-slice_fusion.1
  42.8 2.4 compare_and_fusion
  45.1 1.7 pad_add_fusion
  46.8 61.9 %all-to-all-done = bf16[8,6,64,512]{3,2,1,0:T(8,128)(2,1)} async-done(((bf16[8,6,64,512]{3,2,1,0:T(8,128)(2,1)}), bf16[8,6,64,512]{3,2,1,0:T(8,128)(2,1)}, u32[]{:S(2)}, u32[]{:S(2)}) %all-to-all-start) | async-done | bytes 3145760 | tf_op jit(solution)/shard_map/all_to_all | solution.py:92
  108.7 4.4 %gather_fusion.1 = bf16[48,64,512]{2,1,0:T(8,128)(2,1)} fusion(bf16[48,64,512]{2,1,0:T(8,128)(2,1)} %bitcast.3, s32[1024]{0:T(1024)S(1)} %pad_clamp_fusion), kind=kCustom, calls=%fused_computation.1 | custom fusion | bytes 6291648 | tf_op jit(solution)/shard_map/gather | solution.py:93
  113.2 4.0 %fusion.49 = (bf16[48,64,256]{2,1,0:T(8,128)(2,1)}, bf16[48,64,256]{2,1,0:T(8,128)(2,1)}) fusion(bf16[48,64,512]{2,1,0:T(8,128)(2,1)} %gather_fusion.1), kind=kLoop, calls=%fused_computation.100 | loop fusion | bytes 6291456 | tf_op jit(solution)/shard_map/slice | solution.py:95
  117.2 2.7 copy.30
  119.8 8.7 %fusion.8 = f32[3584,512,2]{1,0,2:T(8,128)} fusion(bf16[512,256]{1,0:T(8,128)(2,1)S(1)} %get-tuple-element.24, bf16[3072,256]{1,0:T(8,128)(2,1)} %bitcast.51, bf16[64,2,8,256]{3,2,1,0:T(8,128)(2,1)S(1)} %bitcast.53), kind=kOutput, calls=%fused_computation.19 | convolution fusion | flops 1882718208 | bytes 17039360 | tf_op jit(solution)/shard_map/rhd,kd->hrk/dot_general | solution.py:104
  128.6 17.1 %fusion.51 = (f32[2,512]{1,0:T(2,128)S(1)}, f32[2,512,3584]{1,2,0:T(8,128)}) fusion(f32[3584,512,2]{1,0,2:T(8,128)} %fusion.8, pred[512,3584]{0,1:T(8,128)(4,1)} %pad_add_fusion), kind=kOutput, calls=%fused_computation.102 | output fusion | flops 22023680 | bytes 31199232 | tf_op jit(solution)/shard_map/sub | solution.py:109
  145.6 7.7 %fusion.11 = bf16[256,2,512]{2,0,1:T(8,128)(2,1)S(1)} fusion(f32[2,512,3584]{1,2,0:T(8,128)} %get-tuple-element.21, f32[2,512]{1,0:T(2,128)S(1)} %get-tuple-element.20, bf16[512,256]{0,1:T(8,128)(2,1)S(1)} %copy.35, bf16[3072,256]{0,1:T(8,128)(2,1)} %copy.30), kind=kOutput, calls=%fused_computation.22 | convolution fusion | flops 1890320384 | bytes 17043456 | tf_op jit(solution)/shard_map/hrk,kd->rhd/dot_general | solution.py:111
  153.4 3.2 %fusion.52 = f32[512,2048]{1,0:T(8,128)} fusion(bf16[512,512]{0,1:T(8,128)(2,1)S(1)} %bitcast.54, bf16[512,2048]{1,0:T(8,128)(2,1)S(1)} %copy-done), kind=kOutput, calls=%fused_computation.103 | convolution fusion | flops 1073741824 | bytes 6815744 | tf_op jit(solution)/shard_map/dot_general | solution.py:113
  157.3 84.0 %all-reduce.3.cloned.1.call-done = f32[512,2048]{1,0:T(8,128)} async-done(((f32[512,2048]{1,0:T(8,128)}), f32[512,2048]{1,0:T(8,128)}) %all-reduce.3.cloned.1.call-update) | async-done | bytes 4194320 | tf_op jit(solution)/shard_map/psum | solution.py:115
  241.3 2.5 multiply_reduce_fusion
  243.9 1.5 add_convert_fusion.1
  245.3 1.1 fusion.53
  246.5 33.5 %all-reduce.5.cloned.1.call-done = f32[512,256]{1,0:T(8,128)} async-done(((f32[512,256]{1,0:T(8,128)}), f32[512,256]{1,0:T(8,128)}) %all-reduce.5.cloned.1.call-update) | async-done | bytes 524304 | tf_op jit(solution)/shard_map/psum | solution.py:124
  279.9 2.7 multiply_reduce_fusion.1
  282.6 2.6 copy.33
  285.2 5.7 %psum.23 = f32[512]{0:T(512)S(1)} all-reduce(f32[512]{0:T(512)S(1)} %get-tuple-element.22), channel_id=1, replica_groups=mesh['req'=8,'tp'=4] {'tp'}, use_global_device_ids=true, to_apply=%region_14.16 | all-reduce | flops 512 | bytes 4096 | tf_op jit(solution)/shard_map/psum | solution.py:129
  290.9 2.2 add_convert_fusion
  (66 shorter events, 3.8 us)
Async XLA Ops:
  6.5 146.8 %copy-start = (bf16[512,2048]{1,0:T(8,128)(2,1)S(1)}, bf16[512,2048]{1,0:T(8,128)(2,1)}, u32[]{:S(2)}) copy-start(bf16[512,2048]{1,0:T(8,128)(2,1)} %param.25) | copy-start | bytes 6291460
  9.3 13.7 %collective-permute-start = (s32[1,6]{0,1:T(8,128)S(1)}, s32[1,6]{0,1:T(8,128)S(1)}, u32[]{:S(2)}, u32[]{:S(2)}) collective-permute-start(s32[1,6]{0,1:T(8,128)S(1)} %get-tuple-element.17), channel_id=1, source_target_pairs={{0,28},{4,0},{8,4},{12,8},{16,12},{20,16},{24,20},{28,24},{1,29},{... | collective-permute-start | bytes 80 | tf_op jit(solution)/shard_map/ppermute | solution.py:18
  15.3 9.5 %collective-permute-start.1 = (s32[1,6]{0,1:T(8,128)S(1)}, s32[1,6]{0,1:T(8,128)S(1)}, u32[]{:S(2)}, u32[]{:S(2)}) collective-permute-start(s32[1,6]{0,1:T(8,128)S(1)} %get-tuple-element.16), channel_id=1, source_target_pairs={{0,24},{4,28},{8,0},{12,4},{16,8},{20,12},{24,16},{28,20},{1,25},{... | collective-permute-start | bytes 80 | tf_op jit(solution)/shard_map/ppermute | solution.py:18
  15.8 10.2 %collective-permute-start.2 = (s32[1,6]{0,1:T(8,128)S(1)}, s32[1,6]{0,1:T(8,128)S(1)}, u32[]{:S(2)}, u32[]{:S(2)}) collective-permute-start(s32[1,6]{0,1:T(8,128)S(1)} %get-tuple-element.15), channel_id=1, source_target_pairs={{0,20},{4,24},{8,28},{12,0},{16,4},{20,8},{24,12},{28,16},{1,21},{... | collective-permute-start | bytes 80 | tf_op jit(solution)/shard_map/ppermute | solution.py:18
  15.8 10.2 %collective-permute-start.3 = (s32[1,6]{0,1:T(8,128)S(1)}, s32[1,6]{0,1:T(8,128)S(1)}, u32[]{:S(2)}, u32[]{:S(2)}) collective-permute-start(s32[1,6]{0,1:T(8,128)S(1)} %get-tuple-element.14), channel_id=1, source_target_pairs={{0,16},{4,20},{8,24},{12,28},{16,0},{20,4},{24,8},{28,12},{1,17},{... | collective-permute-start | bytes 80 | tf_op jit(solution)/shard_map/ppermute | solution.py:18
  18.7 7.2 %collective-permute-start.4 = (s32[1,6]{0,1:T(8,128)S(1)}, s32[1,6]{0,1:T(8,128)S(1)}, u32[]{:S(2)}, u32[]{:S(2)}) collective-permute-start(s32[1,6]{0,1:T(8,128)S(1)} %get-tuple-element.13), channel_id=1, source_target_pairs={{0,12},{4,16},{8,20},{12,24},{16,28},{20,0},{24,4},{28,8},{1,13},{... | collective-permute-start | bytes 80 | tf_op jit(solution)/shard_map/ppermute | solution.py:18
  23.0 6.4 %collective-permute-start.5 = (s32[1,6]{0,1:T(8,128)S(1)}, s32[1,6]{0,1:T(8,128)S(1)}, u32[]{:S(2)}, u32[]{:S(2)}) collective-permute-start(s32[1,6]{0,1:T(8,128)S(1)} %get-tuple-element.12), channel_id=1, source_target_pairs={{0,8},{4,12},{8,16},{12,20},{16,24},{20,28},{24,0},{28,4},{1,9},{5... | collective-permute-start | bytes 80 | tf_op jit(solution)/shard_map/ppermute | solution.py:18
  24.8 6.3 %collective-permute-start.6 = (s32[1,6]{0,1:T(8,128)S(1)}, s32[1,6]{0,1:T(8,128)S(1)}, u32[]{:S(2)}, u32[]{:S(2)}) collective-permute-start(s32[1,6]{0,1:T(8,128)S(1)} %get-tuple-element.11), channel_id=1, source_target_pairs={{0,4},{4,8},{8,12},{12,16},{16,20},{20,24},{24,28},{28,0},{1,5},{5... | collective-permute-start | bytes 80 | tf_op jit(solution)/shard_map/ppermute | solution.py:18
  36.0 4.7 %copy-start.8 = (s32[1,8]{1,0:T(1,128)S(1)}, s32[1,8]{1,0:T(1,128)}, u32[]{:S(2)}) copy-start(s32[1,8]{1,0:T(1,128)} %param.33) | copy-start | bytes 100
  36.0 4.9 %copy-start.10 = (s32[1,8]{1,0:T(1,128)S(1)}, s32[1,8]{1,0:T(1,128)}, u32[]{:S(2)}) copy-start(s32[1,8]{1,0:T(1,128)} %param.35) | copy-start | bytes 100
  36.0 5.0 %copy-start.4 = (bf16[512,512]{1,0:T(8,128)(2,1)S(1)}, bf16[512,512]{1,0:T(8,128)(2,1)}, u32[]{:S(2)}) copy-start(bf16[512,512]{1,0:T(8,128)(2,1)} %param.21) | copy-start | bytes 1572868
  36.0 6.2 %copy-start.9 = (s32[48,1]{0,1:T(1,128)S(1)}, s32[48,1]{0,1:T(1,128)}, u32[]{:S(2)}) copy-start(s32[48,1]{0,1:T(1,128)} %param.31) | copy-start | bytes 580
  36.0 6.3 %copy-start.7 = (s32[1,8]{1,0:T(1,128)S(1)}, s32[1,8]{1,0:T(1,128)}, u32[]{:S(2)}) copy-start(s32[1,8]{1,0:T(1,128)} %param.34) | copy-start | bytes 100
  36.0 72.7 %all-to-all-start = ((bf16[8,6,64,512]{3,2,1,0:T(8,128)(2,1)}), bf16[8,6,64,512]{3,2,1,0:T(8,128)(2,1)}, u32[]{:S(2)}, u32[]{:S(2)}) async-start(bf16[8,6,64,512]{3,2,1,0:T(8,128)(2,1)} %bitcast.50), calls=%async_computation | async-start | bytes 6291456 | tf_op jit(solution)/shard_map/all_to_all | solution.py:92
  40.6 200.7 %all-reduce.3.cloned.1.call-start = ((), (), s32[]{:S(2)}) async-start(), calls=%async_computation.1 | async-start | bytes 8388608 | tf_op jit(solution)/shard_map/psum | solution.py:115
  117.2 2.7 copy-start.1
  156.6 0.7 copy-start.5
  156.7 87.2 %copy-start.2 = (bf16[512,512]{1,0:T(8,128)(2,1)S(1)}, bf16[512,512]{1,0:T(8,128)(2,1)}, u32[]{:S(2)}) copy-start(bf16[512,512]{1,0:T(8,128)(2,1)} %param.19) | copy-start | bytes 1572868
  156.7 123.3 %all-reduce.5.cloned.1.call-start = ((), (), s32[]{:S(2)}) async-start(), calls=%async_computation.2 | async-start | bytes 1048576 | tf_op jit(solution)/shard_map/psum | solution.py:124
  157.3 88.0 %copy-start.3 = (bf16[512,256]{1,0:T(8,128)(2,1)S(1)}, bf16[512,256]{1,0:T(8,128)(2,1)}, u32[]{:S(2)}) copy-start(bf16[512,256]{1,0:T(8,128)(2,1)} %param.28) | copy-start | bytes 786436
  157.3 89.1 %copy-start.6 = (bf16[512]{0:T(512)(128)(2,1)S(1)}, bf16[512]{0:T(512)(128)(2,1)}, u32[]{:S(2)}) copy-start(bf16[512]{0:T(512)(128)(2,1)} %param.30) | copy-start | bytes 3076
Sparse Core Ops, SparseCore 0:
  156.8 84.4 all-reduce.2
  246.6 33.3 all-reduce.4
